TPU v7x, 512 devices: a whole 4x8x8 slice. The times are simulated.
512 devices in a mesh: dp: 16 (over y, core), cell: 32 (over x, z).
Axes of the slice: x: 4, y: 8, z: 8, core: 2. Of those that a mesh axis runs over, the one named last changes fastest.
Arguments:
- sensitivity: bfloat16 [2048, 200704], P('dp', 'cell'), may hold values from -0.0390625 to 0.0390625
- direction: bfloat16 [16, 200704], P(None, 'cell'), may hold values from -6 to 6
- depth_weight: float32 [200704], P('cell'), may hold values from 0.3 to 3
- counts: int32 [32], P('cell'), may hold values from 4704 to 6272, as said below
- send_lists: int32 [32, 2, 128], P('cell'), may hold values from 0 to 6271, as said below
- neighbours: int32 [6, 200704], P(None, 'cell'), may hold values from 0 to 6528, as said below
Outputs:
- product: float32 [16, 200704], P(None, 'cell')
Inputs may be any that keep to these rules, and one draw needn't show every extreme that they name: `counts`: every partition has at least 4704 live cells; some partition is full in every draw. `send_lists`: entries are local indices of live cells of their own partition. `neighbours`: entries below 6272 are live local cells that differ from the cell's own local index by at most 64; 6272 to 6527 name received rim cells; 6528 is an absent face; padded slots hold only absent faces.
All inputs are finite; a program needn't handle non-finite values.
Results may differ from a plain program's by a relative error of at most 0.0008.
Values sent between devices are 32-bit elements; how exact they have to be, the bound alone decides.
No kernel may reach another device: no remote copies, remote signals or barrier semaphores. Data moves between devices by JAX's collectives and lax.ppermute only.
A program may use at most 64 MiB of HBM per device.

v0:
```python
import jax
import jax.numpy as jnp
from jax import lax
from jax.sharding import PartitionSpec as P


def padded_2(value, sides, width):
    for axis, dim in sides:
        count, length = (lax.axis_size(axis), value.shape[dim])
        up = [(i, (i + 1) % count) for i in range(count - 1)]
        down = [(j, i) for i, j in up]
        last = lax.slice_in_dim(value, length - width, length, axis=dim)
        leading = lax.slice_in_dim(value, 0, width, axis=dim)
        before = lax.ppermute(last, axis, up)
        after = lax.ppermute(leading, axis, down)
        value = jnp.concatenate([before, value, after], axis=dim)
    return value


def pick_block():
    block_len = 8
    for candidate in range(128, 7, -8):
        block_len = candidate
        break
    return block_len


def pick_group(block_count):
    group_len = 1
    for candidate in range(1, 9):
        if block_count % candidate == 0:
            group_len = candidate
    return group_len


def smoothness(masked_f, weight, send_lists, neighbours, width):
    slots = masked_f.shape[1]
    values = jnp.concatenate([masked_f * weight[None, :], weight[None, :]], axis=0)
    picked = jnp.take(values, send_lists[0].reshape(-1), axis=1)
    rim = picked.shape[1] // 2
    padded = padded_2(picked, (("cell", 1),), rim)
    rim_vals = jnp.concatenate([padded[:, :rim], padded[:, 3 * rim :]], axis=1)
    lanes = values.shape[0]
    block_len = pick_block()
    block_count = width // block_len
    pieces = 1 + (128 + block_len - 1) // block_len
    spread = jnp.pad(values, ((0, 0), (64, pieces * block_len)))
    local_vals = lax.slice_in_dim(spread, 0, (block_count + pieces - 1) * block_len, axis=1)
    shifted = [
        local_vals[:, m * block_len : (m + block_count) * block_len].reshape(
            lanes, block_count, block_len
        )
        for m in range(pieces)
    ]
    rim_part = jnp.broadcast_to(rim_vals[:, None, :], (lanes, block_count, 2 * rim))
    windows = jnp.concatenate(shifted + [rim_part], axis=2).transpose(1, 0, 2)
    span = windows.shape[2]
    position = jnp.arange(width, dtype=jnp.int32)
    anchor = position // block_len * block_len
    column = jnp.where(
        neighbours < slots,
        neighbours - anchor[None, :] + 64,
        jnp.where(neighbours < slots + 2 * rim, pieces * block_len + neighbours - slots, -1),
    )
    column = column.reshape(neighbours.shape[0], block_count, block_len).transpose(1, 0, 2)
    group_len = pick_group(block_count)
    windows = windows.reshape(block_count // group_len, group_len, lanes, span)
    column = column.reshape(block_count // group_len, group_len, neighbours.shape[0], block_len)

    def gather_block(item):
        window_set, column_set = item
        target = jnp.arange(span, dtype=jnp.int32)[None, None, :, None]
        hits = jnp.sum((column_set[:, :, None, :] == target).astype(jnp.float32), axis=1)
        return jnp.einsum("grw,gwb->grb", window_set, hits, precision=lax.Precision.HIGHEST)

    sums = lax.map(gather_block, (windows, column))
    sums = sums.reshape(block_count, lanes, block_len).transpose(1, 0, 2).reshape(lanes, width)
    coupling = masked_f * sums[-1][None, :] - sums[:-1]
    return weight[None] * weight[None] * masked_f + weight[None] * coupling


def on_device(sensitivity, direction, depth_weight, counts, send_lists, neighbours):
    slots = sensitivity.shape[1]
    nvecs = direction.shape[0]
    live = jnp.arange(slots, dtype=jnp.int32) < counts[0]
    masked = jnp.where(live[None, :], direction, jnp.zeros_like(direction))
    partial_data = lax.dot_general(
        masked, sensitivity, (((1,), (1,)), ((), ())), preferred_element_type=jnp.float32
    )
    summed = lax.psum(partial_data, "cell")
    rounded = summed.astype(jnp.bfloat16)
    remainder = (summed - rounded.astype(jnp.float32)).astype(jnp.bfloat16)
    stacked = jnp.concatenate([rounded, remainder], axis=0)
    both = jnp.dot(stacked, sensitivity, preferred_element_type=jnp.float32)
    partial_cells = both[:nvecs] + both[nvecs:]
    weight = jnp.where(live, depth_weight, jnp.float32(0.0))
    masked_f = masked.astype(jnp.float32)
    misfit = lax.psum(partial_cells, "dp")
    smooth = smoothness(masked_f, weight, send_lists, neighbours, slots)
    total = misfit + 0.5 * smooth
    return jnp.where(live[None, :], total, jnp.float32(0.0))


def solution(mesh):
    placed = (
        P("dp", "cell"),
        P(None, "cell"),
        P("cell"),
        P("cell"),
        P("cell", None, None),
        P(None, "cell"),
    )
    return jax.shard_map(
        on_device, mesh=mesh, in_specs=placed, out_specs=P(None, "cell"), check_vma=False
    )
```

profile of v0, /device:TPU:1, one launch (start us, length us, event | category | flops | bytes accessed | tf_op | source)
XLA Modules:
  0.0 220.8 jit_solution(9854497497350042663)
XLA Ops:
  7.3 0.8 fusion.22
  8.1 1.0 convert_multiply_fusion.1
  9.1 0.1 pad_maximum_fusion.1
  9.2 2.3 %copy.26 = f32[17,6272]{0,1:T(8,128)} copy(f32[17,6272]{1,0:T(8,128)S(1)} %pad_maximum_fusion.1) | data formatting | bytes 852992 | tf_op jit(solution)/shard_map/concatenate | solution.py:38
  11.6 2.6 %gather_fusion = f32[256,17]{1,0:T(8,128)S(1)} fusion(f32[17,6272]{0,1:T(8,128)} %copy.26, s32[1024]{0:T(1024)S(1)} %pad_clamp_fusion), kind=kCustom, calls=%fused_computation | custom fusion | bytes 35840 | tf_op jit(solution)/shard_map/jit(_take)/gather | solution.py:39
  14.2 0.1 select_bitcast_fusion
  14.3 0.7 fusion.23
  14.9 5.4 %collective-permute-start = (f32[17,128]{0,1:T(8,128)}, f32[17,128]{0,1:T(8,128)}, u32[]{:S(2)}, u32[]{:S(2)}) collective-permute-start(f32[17,128]{0,1:T(8,128)} %get-tuple-element.42), channel_id=1, source_target_pairs={{0,1},{1,2},{2,3},{3,4},{4,5},{5,6},{6,7},{7,8},{8,9},{9,10},{10,1... | collective-permute-start | bytes 26120 | tf_op jit(solution)/shard_map/ppermute | solution.py:14
  20.4 1.3 collective-permute-start.1
  21.7 0.5 fusion.10
  22.2 67.6 %psum.14 = f32[16,128]{1,0:T(8,128)S(1)} all-reduce(f32[16,128]{1,0:T(8,128)S(1)} %fusion.10), channel_id=1, replica_groups=mesh['dp'=16,'cell'=32] {'cell'}, use_global_device_ids=true, to_apply=%region_0.1 | all-reduce | flops 2048 | bytes 16384 | tf_op jit(solution)/shard_map/psum | solution.py:90
  89.8 0.4 fusion.16
  90.1 0.8 slice_add_fusion
  91.0 0.7 select_select_fusion
  91.7 0.4 pad_slice_fusion.1
  92.1 0.8 reshape.80
  92.9 1.1 copy.29
  94.1 0.1 reshape.81
  94.1 0.1 copy.30
  94.2 0.9 copy.27
  95.2 0.1 copy.28
  95.3 0.1 broadcast_in_dim.71
  95.4 1.7 pad_maximum_fusion
  97.1 30.0 %while.10 = (s32[]{:T(128)}, f32[7,7,17,128]{3,2,1,0:T(8,128)S(1)}, f32[7,7,17,512]{3,2,1,0:T(8,128)}, s32[7,7,6,128]{3,2,1,0:T(8,128)}, s32[]{:T(128)}) while((s32[]{:T(128)}, f32[7,7,17,128]{3,2,1,0:T(8,128)S(1)}, f32[7,7,17,512]{3,2,1,0:T(8,128)}, s32[7,7,6,128]{3,2,1,0:T(8,128)}, s32[]{:T(128)}) %tuple.29), condition=%wide.region_4.5_spmd, body=%wide.region_2.4_spmd.sunk | while | flops 101384192 | bytes 4165697 | solution.py:76
  97.1 0.8 dynamic-slice_bitcast_fusion.2
  97.9 1.5 convert_reduce_fusion.2
  99.4 2.0 fusion.32
  101.4 0.8 dynamic-slice_bitcast_fusion.2
  102.2 1.5 convert_reduce_fusion.2
  103.7 2.0 fusion.32
  105.7 0.8 dynamic-slice_bitcast_fusion.2
  106.5 1.5 convert_reduce_fusion.2
  107.9 2.0 fusion.32
  110.0 0.8 dynamic-slice_bitcast_fusion.2
  110.8 1.5 convert_reduce_fusion.2
  112.2 2.0 fusion.32
  114.3 0.8 dynamic-slice_bitcast_fusion.2
  115.0 1.5 convert_reduce_fusion.2
  116.5 2.0 fusion.32
  118.6 0.8 dynamic-slice_bitcast_fusion.2
  119.3 1.5 convert_reduce_fusion.2
  120.8 2.0 fusion.32
  122.8 0.8 dynamic-slice_bitcast_fusion.2
  123.6 1.5 convert_reduce_fusion.2
  125.1 2.0 fusion.32
  127.1 0.1 copy.36
  127.3 84.8 %all-reduce.3.cloned.1.call-done = f32[16,6272]{1,0:T(8,128)} async-done(((f32[16,6272]{1,0:T(8,128)}), f32[16,6272]{1,0:T(8,128)}) %all-reduce.3.cloned.1.call-update) | async-done | bytes 401424 | tf_op jit(solution)/shard_map/psum | solution.py:98
  212.1 1.9 fusion.7
  (27 shorter events, 0.2 us)
Async XLA Ops:
  6.5 15.1 %copy-start = (bf16[128,6272]{1,0:T(8,128)(2,1)S(1)}, bf16[128,6272]{1,0:T(8,128)(2,1)}, u32[]{:S(2)}) copy-start(bf16[128,6272]{1,0:T(8,128)(2,1)} %param.8) | copy-start | bytes 4816900
  6.5 205.5 %all-reduce.3.cloned.1.call-start = ((), (), s32[]{:S(2)}) async-start(), calls=%async_computation | async-start | bytes 802816 | tf_op jit(solution)/shard_map/psum | solution.py:98
  9.1 2.4 %copy-start.5 = (s32[1,2,128]{2,1,0:T(2,128)S(1)}, s32[1,2,128]{2,1,0:T(2,128)}, u32[]{:S(2)}) copy-start(s32[1,2,128]{2,1,0:T(2,128)} %param.12) | copy-start | bytes 3076
  9.2 12.5 %copy-start.1 = (bf16[16,6272]{1,0:T(8,128)(2,1)S(1)}, bf16[16,6272]{1,0:T(8,128)(2,1)}, u32[]{:S(2)}) copy-start(bf16[16,6272]{1,0:T(8,128)(2,1)} %param.9) | copy-start | bytes 602116
  14.9 79.3 %collective-permute-start = (f32[17,128]{0,1:T(8,128)}, f32[17,128]{0,1:T(8,128)}, u32[]{:S(2)}, u32[]{:S(2)}) collective-permute-start(f32[17,128]{0,1:T(8,128)} %get-tuple-element.42), channel_id=1, source_target_pairs={{0,1},{1,2},{2,3},{3,4},{4,5},{5,6},{6,7},{7,8},{8,9},{9,10},{10,1... | collective-permute-start | bytes 26120 | tf_op jit(solution)/shard_map/ppermute | solution.py:14
  20.4 74.8 %collective-permute-start.1 = (f32[17,128]{0,1:T(8,128)}, f32[17,128]{0,1:T(8,128)S(1)}, u32[]{:S(2)}, u32[]{:S(2)}) collective-permute-start(f32[17,128]{0,1:T(8,128)} %get-tuple-element.43), channel_id=1, source_target_pairs={{1,0},{2,1},{3,2},{4,3},{5,4},{6,5},{7,6},{8,7},{9,8},{10,9},{11,1... | collective-permute-start | bytes 26120 | tf_op jit(solution)/shard_map/ppermute | solution.py:15
  22.2 68.8 %copy-start.4 = (s32[6,6272]{1,0:T(8,128)S(1)}, s32[6,6272]{1,0:T(8,128)}, u32[]{:S(2)}) copy-start(s32[6,6272]{1,0:T(8,128)} %param.13) | copy-start | bytes 451588
  95.4 1.8 copy-start.3
  97.1 115.0 %copy-start.2 = (bf16[16,6272]{1,0:T(8,128)(2,1)S(1)}, bf16[16,6272]{1,0:T(8,128)(2,1)}, u32[]{:S(2)}) copy-start(bf16[16,6272]{1,0:T(8,128)(2,1)} %param.9) | copy-start | bytes 602116
Sparse Core Ops, SparseCore 0:
  91.1 120.9 all-reduce.2
where the time goes:
time: 222 us; the launch traced here: 221 us
  waiting for transfers between devices  84.8 us (38%)
  blocking collectives  67.6 us (30%)
  other arithmetic  17.4 us (8%)
  matrix products  15 us (7%)
  local copies, waits for them, and re-layouts  14.7 us (7%)
  between operations  14.4 us (6%)
  starting transfers between devices  6.7 us (3%)
    psum x1, waiting for transfers between devices, on_device(): misfit = lax.psum(partial_cells, 'dp')  84.8 us
    psum x1, blocking collectives, on_device(): summed = lax.psum(partial_data, 'cell')  67.6 us
    dot_general x7, matrix products, gather_block(): jnp.einsum('grw,gwb->grb', window_set, hits, precision=lax.Precision.HIGH...  14.2 us
    reduce_sum x7, other arithmetic, gather_block(): jnp.sum((column_set[:, :, None, :] == target).astype(jnp.float32), axis=1)  10.3 us
    ppermute x1, starting transfers between devices, padded_2(): before = lax.ppermute(last, axis, up)  5.42 us
    eq x7, local copies, waits for them, and re-layouts, gather_block(): column_set[:, :, None, :] == target  5.32 us
  transfers between devices with their start and end apart: 3, of which 1 were waited for; matrix products, arithmetic and copies ran while one was open for 17% of the time, Pallas kernels for 0%

commit v1 on v0

--- a/solution.py
+++ b/solution.py
@@ -1,7 +1,15 @@
+import functools
 import jax
 import jax.numpy as jnp
 from jax import lax
 from jax.sharding import PartitionSpec as P
+
+
+def shapes_replace(load, axis_name):
+    return jnp.sum(lax.all_gather(load, axis_name), 0)
+
+
+load_regions_for = functools.partial(shapes_replace, axis_name="dp")
 
 
 def padded_2(value, sides, width):
@@ -95,7 +103,7 @@
     partial_cells = both[:nvecs] + both[nvecs:]
     weight = jnp.where(live, depth_weight, jnp.float32(0.0))
     masked_f = masked.astype(jnp.float32)
-    misfit = lax.psum(partial_cells, "dp")
+    misfit = load_regions_for(partial_cells)
     smooth = smoothness(masked_f, weight, send_lists, neighbours, slots)
     total = misfit + 0.5 * smooth
     return jnp.where(live[None, :], total, jnp.float32(0.0))

time: 222 us -> 153 us (0.69)
  the two profiles are of different devices: /device:TPU:1 before, /device:TPU:32 now
where the time goes in v1:
time: 153 us; the launch traced here: 152 us
  blocking collectives  82 us (54%)
  other arithmetic  18 us (12%)
  matrix products  16 us (10%)
  local copies, waits for them, and re-layouts  15.4 us (10%)
  between operations  14.4 us (9%)
  starting transfers between devices  5.83 us (4%)
    psum x1, blocking collectives, on_device(): summed = lax.psum(partial_data, 'cell')  82 us
    dot_general x7, matrix products, gather_block(): jnp.einsum('grw,gwb->grb', window_set, hits, precision=lax.Precision.HIGH...  14.2 us
    reduce_sum x7, other arithmetic, gather_block(): jnp.sum((column_set[:, :, None, :] == target).astype(jnp.float32), axis=1)  10.3 us
    eq x7, local copies, waits for them, and re-layouts, gather_block(): column_set[:, :, None, :] == target  5.3 us
    ppermute x1, starting transfers between devices, padded_2(): before = lax.ppermute(last, axis, up)  4.55 us
    reduce_sum x1, other arithmetic, shapes_replace(): return jnp.sum(lax.all_gather(load, axis_name), 0)  3.23 us
  transfers between devices with their start and end apart: 3, of which 0 were waited for; matrix products, arithmetic and copies ran while one was open for 28% of the time, Pallas kernels for 0%

profile of v1, /device:TPU:32, one launch (start us, length us, event | category | flops | bytes accessed | tf_op | source)
XLA Modules:
  0.0 152.0 jit_solution(8363669606918623620)
XLA Ops:
  7.3 0.6 copy-done
  8.0 1.4 fusion.10
  9.4 82.0 %psum.7 = f32[16,128]{1,0:T(8,128)S(1)} all-reduce(f32[16,128]{1,0:T(8,128)S(1)} %fusion.10), channel_id=1, replica_groups=mesh['dp'=16,'cell'=32] {'cell'}, use_global_device_ids=true, to_apply=%region_0.1 | all-reduce | flops 2048 | bytes 16384 | tf_op jit(solution)/shard_map/psum | solution.py:98
  91.5 0.4 fusion.16
  91.8 0.8 slice_add_fusion
  92.7 0.1 convert_multiply_fusion.1
  92.8 0.1 pad_maximum_fusion.1
  92.9 2.4 %copy.37 = f32[17,6272]{0,1:T(8,128)} copy(f32[17,6272]{1,0:T(8,128)S(1)} %pad_maximum_fusion.1) | data formatting | bytes 852992 | tf_op jit(solution)/shard_map/concatenate | solution.py:46
  95.3 2.6 %gather_fusion = f32[256,17]{1,0:T(8,128)S(1)} fusion(f32[17,6272]{0,1:T(8,128)} %copy.37, s32[1024]{0:T(1024)S(1)} %pad_clamp_fusion), kind=kCustom, calls=%fused_computation | custom fusion | bytes 35840 | tf_op jit(solution)/shard_map/jit(_take)/gather | solution.py:47
  97.9 0.1 select_bitcast_fusion
  98.1 0.7 fusion.23
  98.7 1.3 collective-permute-start.1
  100.0 4.5 %collective-permute-start = (f32[17,128]{0,1:T(8,128)}, f32[17,128]{0,1:T(8,128)S(1)}, u32[]{:S(2)}, u32[]{:S(2)}) collective-permute-start(f32[17,128]{0,1:T(8,128)} %get-tuple-element.42), channel_id=1, source_target_pairs={{0,1},{1,2},{2,3},{3,4},{4,5},{5,6},{6,7},{7,8},{8,9},{9,10},{10,1... | collective-permute-start | bytes 26120 | tf_op jit(solution)/shard_map/ppermute | solution.py:22
  104.6 0.7 select_select_fusion
  105.3 0.4 pad_slice_fusion.1
  105.7 0.8 reshape.81
  106.5 1.1 copy.41
  107.7 0.1 reshape.80
  107.7 0.1 copy.40
  107.9 0.9 copy.39
  108.8 0.1 copy.38
  108.9 0.1 broadcast_in_dim.71
  109.0 1.8 %pad_maximum_fusion = f32[17,49,512]{2,0,1:T(8,128)} fusion(f32[17,49,256]{2,0,1:T(8,128)S(1)} %broadcast_in_dim.71, f32[17,49,128]{2,0,1:T(8,128)S(1)} %copy.41, f32[17,49,128]{2,0,1:T(8,128)S(1)} %copy.40), kind=kLoop, calls=%fused_computation.9 | loop fusion | flops 852992 | bytes 3411968 | tf_op jit(solution)/shard_map/concatenate | solution.py:64
  110.8 30.0 %while.10 = (s32[]{:T(128)}, f32[7,7,17,128]{3,2,1,0:T(8,128)S(1)}, f32[7,7,17,512]{3,2,1,0:T(8,128)}, s32[7,7,6,128]{3,2,1,0:T(8,128)}, s32[]{:T(128)}) while((s32[]{:T(128)}, f32[7,7,17,128]{3,2,1,0:T(8,128)S(1)}, f32[7,7,17,512]{3,2,1,0:T(8,128)}, s32[7,7,6,128]{3,2,1,0:T(8,128)}, s32[]{:T(128)}) %tuple.29), condition=%wide.region_4.5_spmd, body=%wide.region_2.4_spmd.sunk | while | flops 101384192 | bytes 4165705 | solution.py:84
  110.8 0.8 dynamic-slice_bitcast_fusion.2
  111.5 1.5 convert_reduce_fusion.2
  113.0 2.0 %fusion.32 = f32[7,7,17,128]{3,2,1,0:T(8,128)S(1)} fusion(f32[7,7,17,128]{3,2,1,0:T(8,128)S(1)} %get-tuple-element.75, s32[]{:T(128)S(6)} %copy.52, f32[7,512,128]{2,1,0:T(8,128)S(1)} %convert_reduce_fusion.2, f32[7,7,17,512]{3,2,1,0:T(8,128)} %get-tuple-element.81), kind=kOutput, calls=%fused_computation.4.clone.1 | convolution fusion | flops 93585408 | bytes 2266112 | tf_op jit(solution)/shard_map/while/body/eval_jaxpr/grw,gwb->grb/dot_general | solution.py:82
  115.0 0.8 dynamic-slice_bitcast_fusion.2
  115.8 1.5 convert_reduce_fusion.2
  117.3 2.0 %fusion.32 = f32[7,7,17,128]{3,2,1,0:T(8,128)S(1)} fusion(f32[7,7,17,128]{3,2,1,0:T(8,128)S(1)} %get-tuple-element.75, s32[]{:T(128)S(6)} %copy.52, f32[7,512,128]{2,1,0:T(8,128)S(1)} %convert_reduce_fusion.2, f32[7,7,17,512]{3,2,1,0:T(8,128)} %get-tuple-element.81), kind=kOutput, calls=%fused_computation.4.clone.1 | convolution fusion | flops 93585408 | bytes 2266112 | tf_op jit(solution)/shard_map/while/body/eval_jaxpr/grw,gwb->grb/dot_general | solution.py:82
  119.3 0.8 dynamic-slice_bitcast_fusion.2
  120.1 1.5 convert_reduce_fusion.2
  121.6 2.0 %fusion.32 = f32[7,7,17,128]{3,2,1,0:T(8,128)S(1)} fusion(f32[7,7,17,128]{3,2,1,0:T(8,128)S(1)} %get-tuple-element.75, s32[]{:T(128)S(6)} %copy.52, f32[7,512,128]{2,1,0:T(8,128)S(1)} %convert_reduce_fusion.2, f32[7,7,17,512]{3,2,1,0:T(8,128)} %get-tuple-element.81), kind=kOutput, calls=%fused_computation.4.clone.1 | convolution fusion | flops 93585408 | bytes 2266112 | tf_op jit(solution)/shard_map/while/body/eval_jaxpr/grw,gwb->grb/dot_general | solution.py:82
  123.6 0.8 dynamic-slice_bitcast_fusion.2
  124.4 1.5 convert_reduce_fusion.2
  125.9 2.0 %fusion.32 = f32[7,7,17,128]{3,2,1,0:T(8,128)S(1)} fusion(f32[7,7,17,128]{3,2,1,0:T(8,128)S(1)} %get-tuple-element.75, s32[]{:T(128)S(6)} %copy.52, f32[7,512,128]{2,1,0:T(8,128)S(1)} %convert_reduce_fusion.2, f32[7,7,17,512]{3,2,1,0:T(8,128)} %get-tuple-element.81), kind=kOutput, calls=%fused_computation.4.clone.1 | convolution fusion | flops 93585408 | bytes 2266112 | tf_op jit(solution)/shard_map/while/body/eval_jaxpr/grw,gwb->grb/dot_general | solution.py:82
  127.9 0.8 dynamic-slice_bitcast_fusion.2
  128.7 1.5 convert_reduce_fusion.2
  130.2 2.0 %fusion.32 = f32[7,7,17,128]{3,2,1,0:T(8,128)S(1)} fusion(f32[7,7,17,128]{3,2,1,0:T(8,128)S(1)} %get-tuple-element.75, s32[]{:T(128)S(6)} %copy.52, f32[7,512,128]{2,1,0:T(8,128)S(1)} %convert_reduce_fusion.2, f32[7,7,17,512]{3,2,1,0:T(8,128)} %get-tuple-element.81), kind=kOutput, calls=%fused_computation.4.clone.1 | convolution fusion | flops 93585408 | bytes 2266112 | tf_op jit(solution)/shard_map/while/body/eval_jaxpr/grw,gwb->grb/dot_general | solution.py:82
  132.2 0.8 dynamic-slice_bitcast_fusion.2
  133.0 1.5 convert_reduce_fusion.2
  134.4 2.0 %fusion.32 = f32[7,7,17,128]{3,2,1,0:T(8,128)S(1)} fusion(f32[7,7,17,128]{3,2,1,0:T(8,128)S(1)} %get-tuple-element.75, s32[]{:T(128)S(6)} %copy.52, f32[7,512,128]{2,1,0:T(8,128)S(1)} %convert_reduce_fusion.2, f32[7,7,17,512]{3,2,1,0:T(8,128)} %get-tuple-element.81), kind=kOutput, calls=%fused_computation.4.clone.1 | convolution fusion | flops 93585408 | bytes 2266112 | tf_op jit(solution)/shard_map/while/body/eval_jaxpr/grw,gwb->grb/dot_general | solution.py:82
  136.5 0.8 dynamic-slice_bitcast_fusion.2
  137.2 1.5 convert_reduce_fusion.2
  138.7 2.0 %fusion.32 = f32[7,7,17,128]{3,2,1,0:T(8,128)S(1)} fusion(f32[7,7,17,128]{3,2,1,0:T(8,128)S(1)} %get-tuple-element.75, s32[]{:T(128)S(6)} %copy.52, f32[7,512,128]{2,1,0:T(8,128)S(1)} %convert_reduce_fusion.2, f32[7,7,17,512]{3,2,1,0:T(8,128)} %get-tuple-element.81), kind=kOutput, calls=%fused_computation.4.clone.1 | convolution fusion | flops 93585408 | bytes 2266112 | tf_op jit(solution)/shard_map/while/body/eval_jaxpr/grw,gwb->grb/dot_general | solution.py:82
  140.8 0.1 copy.48
  141.0 3.2 %reduce_sum.18 = f32[16,6272]{1,0:T(8,128)S(1)} reduce(f32[16,16,6272]{2,1,0:T(8,128)} %bitcast.48, f32[]{:T(128)} %constant.53.clone.1), dimensions={0}, to_apply=%region_1.2 | reduce | flops 1505280 | bytes 6823940 | tf_op jit(solution)/shard_map/reduce_sum | solution.py:9
  144.2 0.9 fusion.7
  (30 shorter events, 0.2 us)
Async XLA Ops:
  6.5 1.4 copy-start
  6.5 134.4 %all-gather.3.cloned.1.call-start = ((), (), s32[]{:S(2)}) async-start(), calls=%async_computation | async-start | bytes 6823936 | tf_op jit(solution)/shard_map/all_gather | solution.py:9
  9.4 83.3 %copy-start.5 = (f32[6272]{0:T(1024)S(1)}, f32[6272]{0:T(1024)}, u32[]{:S(2)}) copy-start(f32[6272]{0:T(1024)} %param.10) | copy-start | bytes 75268
  9.4 83.3 %copy-start.1 = (bf16[16,6272]{1,0:T(8,128)(2,1)S(1)}, bf16[16,6272]{1,0:T(8,128)(2,1)}, u32[]{:S(2)}) copy-start(bf16[16,6272]{1,0:T(8,128)(2,1)} %param.9) | copy-start | bytes 602116
  92.8 2.5 %copy-start.6 = (s32[1,2,128]{2,1,0:T(2,128)S(1)}, s32[1,2,128]{2,1,0:T(2,128)}, u32[]{:S(2)}) copy-start(s32[1,2,128]{2,1,0:T(2,128)} %param.12) | copy-start | bytes 3076
  92.8 11.7 %copy-start.4 = (s32[6,6272]{1,0:T(8,128)S(1)}, s32[6,6272]{1,0:T(8,128)}, u32[]{:S(2)}) copy-start(s32[6,6272]{1,0:T(8,128)} %param.13) | copy-start | bytes 451588
  98.7 9.2 %collective-permute-start.1 = (f32[17,128]{0,1:T(8,128)}, f32[17,128]{0,1:T(8,128)}, u32[]{:S(2)}, u32[]{:S(2)}) collective-permute-start(f32[17,128]{0,1:T(8,128)} %get-tuple-element.43), channel_id=1, source_target_pairs={{1,0},{2,1},{3,2},{4,3},{5,4},{6,5},{7,6},{8,7},{9,8},{10,9},{11,1... | collective-permute-start | bytes 26120 | tf_op jit(solution)/shard_map/ppermute | solution.py:23
  100.0 8.8 %collective-permute-start = (f32[17,128]{0,1:T(8,128)}, f32[17,128]{0,1:T(8,128)S(1)}, u32[]{:S(2)}, u32[]{:S(2)}) collective-permute-start(f32[17,128]{0,1:T(8,128)} %get-tuple-element.42), channel_id=1, source_target_pairs={{0,1},{1,2},{2,3},{3,4},{4,5},{5,6},{6,7},{7,8},{8,9},{9,10},{10,1... | collective-permute-start | bytes 26120 | tf_op jit(solution)/shard_map/ppermute | solution.py:22
  109.0 1.8 %copy-start.3 = (f32[7,7,17,128]{3,2,1,0:T(8,128)S(1)}, f32[7,7,17,128]{3,2,1,0:T(8,128)}, u32[]{:S(2)}) copy-start(f32[7,7,17,128]{3,2,1,0:T(8,128)} %custom-call.2) | copy-start | bytes 1279492
  140.9 3.2 %copy-start.2 = (bf16[16,6272]{1,0:T(8,128)(2,1)S(1)}, bf16[16,6272]{1,0:T(8,128)(2,1)}, u32[]{:S(2)}) copy-start(bf16[16,6272]{1,0:T(8,128)(2,1)} %param.9) | copy-start | bytes 602116
Sparse Core Ops, SparseCore 0:
  92.8 40.0 all-gather.2
